TPU v7x, 256 devices: a whole 4x4x8 slice. The times are simulated.
256 devices in a mesh: row: 32 (over y, z_hi, x), col: 8 (over z_lo, core).
Axes of the slice: x: 4, y: 4, z: 8 (z_hi: 2, z_lo: 4; z = z_hi * 4 + z_lo), core: 2. Of those that a mesh axis runs over, the one named last changes fastest.
Arguments:
- trailing: float32 [2, 32768, 4096], P(None, 'row', 'col'), may hold values from -6 to 6
- panel: float32 [2, 32768, 256], P(None, ('row', 'col')), may hold values from -4 to 4
- diag_inverse: float32 [2, 256, 256], replicated, as said below
Outputs:
- scaled: float32 [2, 32768, 256], P(None, ('row', 'col'))
- updated: float32 [2, 32768, 4096], P(None, 'row', 'col')
Inputs may be any that keep to these rules, and one draw needn't show every extreme that they name: diag_inverse is complex-symmetric: each part equals its own transpose.
All inputs are finite; a program needn't handle non-finite values.
Results may differ from a plain program's by a relative error of at most 0.00007.
Values sent between devices are 32-bit elements; how exact they have to be, the bound alone decides.
No kernel may reach another device: no remote copies, remote signals or barrier semaphores. Data moves between devices by JAX's collectives and lax.ppermute only.
A program may use at most 64 MiB of HBM per device.

v0:
```python
import jax
import jax.numpy as jnp
from jax import lax
from jax.sharding import Mesh
from jax.sharding import PartitionSpec as P

AXES = ("y", "zh", "x", "zl", "core")
ROW = ("y", "zh", "x")
COL = ("zl", "core")


def complex_product(left, right):
    hp = lax.Precision.HIGHEST
    real_part = jnp.dot(left[0], right[0], precision=hp) - jnp.dot(left[1], right[1], precision=hp)
    imag_part = jnp.dot(left[0], right[1], precision=hp) + jnp.dot(left[1], right[0], precision=hp)
    return jnp.stack([real_part, imag_part])


def product_transposed(left, right):
    hp = lax.Precision.HIGHEST
    dims = (((1,), (1,)), ((), ()))
    real_part = lax.dot_general(left[0], right[0], dims, precision=hp) - lax.dot_general(
        left[1], right[1], dims, precision=hp
    )
    imag_part = lax.dot_general(left[0], right[1], dims, precision=hp) + lax.dot_general(
        left[1], right[0], dims, precision=hp
    )
    return jnp.stack([real_part, imag_part])


def make_local(sizes):
    ny, nh, nx, nl, nc = sizes

    def lin(y, h, x, l, c):
        return (((y * nh + h) * nx + x) * nl + l) * nc + c

    pieces = nl * nc
    transpose = []
    for g in range(nx):
        for l in range(nl):
            for c in range(nc):
                p = nc * l + c
                transpose.append((lin(0, 0, g, l, c), lin(0, 0, p % nx, g, p // nx)))

    def shift(y0, y1, h0, h1):
        return [
            (lin(y0, h0, x, l, c), lin(y1, h1, x, l, c))
            for x in range(nx)
            for l in range(nl)
            for c in range(nc)
        ]

    def local(trailing, panel, diag_inverse):
        scaled = complex_product(panel, diag_inverse)
        block = lax.all_gather(panel, COL, axis=1, tiled=True)
        yi = lax.axis_index("y")
        hi = lax.axis_index("zh")
        piece = lax.ppermute(panel, AXES, transpose)
        r1 = lax.ppermute(piece, AXES, shift(0, 1, 0, 0))
        r3 = lax.ppermute(piece, AXES, shift(0, ny - 1, 0, 0))
        r2 = lax.ppermute(r1, AXES, shift(1, 2, 0, 0))
        along_y = jnp.where(yi == 1, r1, jnp.where(yi == 2, r2, jnp.where(yi == ny - 1, r3, piece)))
        rz = lax.ppermute(along_y, AXES, [pr for y in range(ny) for pr in shift(y, y, 0, 1)])
        held = jnp.where(hi == 0, along_y, rz)
        window = lax.all_gather(held, "x", axis=1, tiled=True)
        tiles = complex_product(window, diag_inverse)
        updated = trailing - product_transposed(block, tiles)
        return (scaled, updated)

    return local


def solution(mesh):
    ny, nh, nx = (4, 2, 4)
    nl, nc = (4, 2)
    devices = mesh.devices.reshape(ny, nh, nx, nl, nc)
    fine = Mesh(devices, AXES)
    return jax.shard_map(
        make_local((ny, nh, nx, nl, nc)),
        mesh=fine,
        in_specs=(P(None, ROW, COL), P(None, ROW + COL, None), P()),
        out_specs=(P(None, ROW + COL, None), P(None, ROW, COL)),
        check_vma=False,
    )
```

profile of v0, /device:TPU:2, one launch (start us, length us, event | category | flops | bytes accessed | tf_op | source)
XLA Modules:
  0.0 150.6 jit_solution(12657731391345822271)
XLA Ops:
  7.2 3.8 %collective-permute-start = (f32[2,128,256]{2,1,0:T(8,128)}, f32[2,128,256]{2,1,0:T(8,128)S(1)}, u32[]{:S(2)}, u32[]{:S(2)}) collective-permute-start(f32[2,128,256]{2,1,0:T(8,128)} %param.4), channel_id=1, source_target_pairs={{0,0},{1,8},{2,16},{3,24},{4,1},{5,9},{6,17},{7,25},{8,2},{9,10},{... | collective-permute-start | bytes 786440 | tf_op jit(solution)/shard_map/ppermute | solution.py:58
  11.0 6.4 %collective-permute-done = f32[2,128,256]{2,1,0:T(8,128)S(1)} collective-permute-done((f32[2,128,256]{2,1,0:T(8,128)}, f32[2,128,256]{2,1,0:T(8,128)S(1)}, u32[]{:S(2)}, u32[]{:S(2)}) %collective-permute-start) | collective-permute-done | bytes 262176 | tf_op jit(solution)/shard_map/ppermute | solution.py:58
  17.5 1.3 collective-permute-start.1
  18.8 1.3 collective-permute-start.3
  20.1 2.5 %collective-permute-done.1 = f32[2,128,256]{2,1,0:T(8,128)S(1)} collective-permute-done((f32[2,128,256]{2,1,0:T(8,128)S(1)}, f32[2,128,256]{2,1,0:T(8,128)S(1)}, u32[]{:S(2)}, u32[]{:S(2)}) %collective-permute-start.1) | collective-permute-done | bytes 262176 | tf_op jit(solution)/shard_map/ppermute | solution.py:59
  22.6 0.7 collective-permute-start.2
  23.3 0.6 collective-permute-done.3
  23.9 0.1 select_select_fusion
  24.0 1.3 collective-permute-start.4
  25.3 3.9 %collective-permute-done.4 = f32[2,128,256]{2,1,0:T(8,128)S(1)} collective-permute-done((f32[2,128,256]{2,1,0:T(8,128)S(1)}, f32[2,128,256]{2,1,0:T(8,128)S(1)}, u32[]{:S(2)}, u32[]{:S(2)}) %collective-permute-start.4) | collective-permute-done | bytes 262176 | tf_op jit(solution)/shard_map/ppermute | solution.py:63
  29.2 0.7 broadcast_select_fusion
  29.9 0.0 all-gather.5.cloned.1.call-start
  30.0 0.7 all-gather.5.cloned.1.call-update
  30.7 5.4 %copy.5 = f32[2,1024,512]{1,2,0:T(8,128)} copy(f32[2,1024,512]{2,1,0:T(8,128)} %param.3) | data formatting | bytes 8388608 | tf_op args[0]
  36.2 0.3 fusion.8
  36.4 0.3 fusion
  36.7 0.3 fusion.14
  37.0 0.3 fusion.1
  37.3 0.7 pad_maximum_fusion
  38.0 45.9 %all-gather.3.cloned.1.call-done = f32[2,512,256]{2,1,0:T(8,128)} async-done(((f32[2,128,256]{2,1,0:T(8,128)}), f32[2,512,256]{2,1,0:T(8,128)}) %all-gather.3.cloned.1.call-update) | async-done | bytes 1048592 | tf_op jit(solution)/shard_map/all_gather | solution.py:65
  84.0 1.7 %fusion.5 = f32[512,256]{1,0:T(8,128)S(1)} fusion(f32[2,512,256]{2,1,0:T(8,128)} %all-gather.3.cloned.1.call-done, f32[2,256,256]{2,1,0:T(8,128)S(1)} %copy-done.1), kind=kOutput, calls=%fused_computation.16 | convolution fusion | flops 402653184 | bytes 1310720 | tf_op jit(solution)/shard_map/dot_general | solution.py:14
  85.7 1.6 %fusion.4 = f32[512,256]{1,0:T(8,128)S(1)} fusion(f32[2,512,256]{2,1,0:T(8,128)} %all-gather.3.cloned.1.call-done, f32[2,256,256]{2,1,0:T(8,128)S(1)} %copy-done.1), kind=kOutput, calls=%fused_computation.15 | convolution fusion | flops 402653184 | bytes 1310720 | tf_op jit(solution)/shard_map/dot_general | solution.py:15
  87.3 0.6 convolution_subtract_fusion
  87.9 0.6 convolution_add_fusion
  88.5 37.6 %all-gather.5.cloned.1.call-done = f32[2,1024,256]{2,1,0:T(8,128)} async-done(((f32[2,128,256]{2,1,0:T(8,128)}), f32[2,1024,256]{2,1,0:T(8,128)}) %all-gather.5.cloned.1.call-update) | async-done | bytes 2097168 | tf_op jit(solution)/shard_map/all_gather | solution.py:55
  126.1 3.2 %fusion.3 = f32[512,1024]{1,0:T(8,128)S(1)} fusion(f32[512,256]{1,0:T(8,128)S(1)} %convolution_subtract_fusion, f32[2,1024,256]{2,1,0:T(8,128)} %all-gather.5.cloned.1.call-done), kind=kOutput, calls=%fused_computation.12 | convolution fusion | flops 1610612736 | bytes 3670016 | tf_op jit(solution)/shard_map/dot_general | solution.py:22
  129.4 1.9 %fusion.2 = f32[512,1024]{1,0:T(8,128)S(1)} fusion(f32[512,256]{1,0:T(8,128)S(1)} %convolution_add_fusion, f32[2,1024,256]{2,1,0:T(8,128)S(1)} %copy-done.2), kind=kOutput, calls=%fused_computation.11 | convolution fusion | flops 1610612736 | bytes 3670016 | tf_op jit(solution)/shard_map/dot_general | solution.py:25
  131.3 2.0 %subtract_bitcast_fusion = f32[1,1024,512]{1,2,0:T(8,128)S(1)} fusion(f32[512,1024]{1,0:T(8,128)S(1)} %fusion.3, f32[512,256]{1,0:T(8,128)S(1)} %convolution_add_fusion, f32[2,1024,256]{2,1,0:T(8,128)S(1)} %copy-done.2), kind=kOutput, calls=%fused_computation.2 | convolution fusion | flops 1611137024 | bytes 5767168 | tf_op jit(solution)/shard_map/dot_general | solution.py:22
  133.3 2.0 %add_bitcast_fusion = f32[1,1024,512]{1,2,0:T(8,128)S(1)} fusion(f32[512,1024]{1,0:T(8,128)S(1)} %fusion.2, f32[512,256]{1,0:T(8,128)S(1)} %convolution_subtract_fusion, f32[2,1024,256]{2,1,0:T(8,128)S(1)} %copy-done.2), kind=kOutput, calls=%fused_computation.1 | convolution fusion | flops 1611137024 | bytes 5767168 | tf_op jit(solution)/shard_map/dot_general | solution.py:25
  135.3 0.2 copy-done
  135.5 2.9 %maximum_subtract_fusion = f32[2,1024,512]{1,2,0:T(8,128)} fusion(f32[2,1024,512]{1,2,0:T(8,128)S(1)} %copy-done, f32[1,1024,512]{1,2,0:T(8,128)S(1)} %add_bitcast_fusion, f32[1,1024,512]{1,2,0:T(8,128)S(1)} %subtract_bitcast_fusion), kind=kLoop, calls=%fused_computation | loop fusion | flops 2097152 | bytes 12582912 | tf_op jit(solution)/shard_map/sub | solution.py:67
  138.4 5.4 %copy.6 = f32[2,1024,512]{2,1,0:T(8,128)} copy(f32[2,1024,512]{1,2,0:T(8,128)} %maximum_subtract_fusion) | data formatting | bytes 8388608
  (12 shorter events, 0.1 us)
Async XLA Ops:
  7.2 76.8 %all-gather.3.cloned.1.call-start = ((), (), s32[]{:S(2)}) async-start(), calls=%async_computation | async-start | bytes 1310720 | tf_op jit(solution)/shard_map/all_gather | solution.py:65
  7.2 10.3 %collective-permute-start = (f32[2,128,256]{2,1,0:T(8,128)}, f32[2,128,256]{2,1,0:T(8,128)S(1)}, u32[]{:S(2)}, u32[]{:S(2)}) collective-permute-start(f32[2,128,256]{2,1,0:T(8,128)} %param.4), channel_id=1, source_target_pairs={{0,0},{1,8},{2,16},{3,24},{4,1},{5,9},{6,17},{7,25},{8,2},{9,10},{... | collective-permute-start | bytes 786440 | tf_op jit(solution)/shard_map/ppermute | solution.py:58
  17.5 5.2 %collective-permute-start.1 = (f32[2,128,256]{2,1,0:T(8,128)S(1)}, f32[2,128,256]{2,1,0:T(8,128)S(1)}, u32[]{:S(2)}, u32[]{:S(2)}) collective-permute-start(f32[2,128,256]{2,1,0:T(8,128)S(1)} %collective-permute-done), channel_id=1, source_target_pairs={{0,64},{1,65},{2,66},{3,67},{4,68},{5,69},{6,70},{7,71},{8,72},{9,... | collective-permute-start | bytes 786440 | tf_op jit(solution)/shard_map/ppermute | solution.py:59
  18.8 5.2 %collective-permute-start.3 = (f32[2,128,256]{2,1,0:T(8,128)S(1)}, f32[2,128,256]{2,1,0:T(8,128)S(1)}, u32[]{:S(2)}, u32[]{:S(2)}) collective-permute-start(f32[2,128,256]{2,1,0:T(8,128)S(1)} %collective-permute-done), channel_id=1, source_target_pairs={{0,192},{1,193},{2,194},{3,195},{4,196},{5,197},{6,198},{7,199},{8... | collective-permute-start | bytes 786440 | tf_op jit(solution)/shard_map/ppermute | solution.py:60
  22.6 1.3 collective-permute-start.2
  24.0 5.2 %collective-permute-start.4 = (f32[2,128,256]{2,1,0:T(8,128)S(1)}, f32[2,128,256]{2,1,0:T(8,128)S(1)}, u32[]{:S(2)}, u32[]{:S(2)}) collective-permute-start(f32[2,128,256]{2,1,0:T(8,128)S(1)} %select_select_fusion), channel_id=1, source_target_pairs={{0,32},{1,33},{2,34},{3,35},{4,36},{5,37},{6,38},{7,39},{8,40},{9,... | collective-permute-start | bytes 786440 | tf_op jit(solution)/shard_map/ppermute | solution.py:63
  29.9 96.2 %all-gather.5.cloned.1.call-start = ((), (), s32[]{:S(2)}) async-start(), calls=%async_computation.1 | async-start | bytes 2359296 | tf_op jit(solution)/shard_map/all_gather | solution.py:55
  30.7 5.5 %copy-start.1 = (f32[2,256,256]{2,1,0:T(8,128)S(1)}, f32[2,256,256]{2,1,0:T(8,128)}, u32[]{:S(2)}) copy-start(f32[2,256,256]{2,1,0:T(8,128)} %param.5) | copy-start | bytes 1572868
  30.7 5.4 %copy-start.4 = (f32[2,128,256]{2,1,0:T(8,128)S(1)}, f32[2,128,256]{2,1,0:T(8,128)}, u32[]{:S(2)}) copy-start(f32[2,128,256]{2,1,0:T(8,128)} %param.4) | copy-start | bytes 786436
  84.0 3.3 %copy-start.3 = (f32[2,512,256]{2,1,0:T(8,128)S(1)}, f32[2,512,256]{2,1,0:T(8,128)}, u32[]{:S(2)}) copy-start(f32[2,512,256]{2,1,0:T(8,128)} %all-gather.3.cloned.1.call-done) | copy-start | bytes 3145732
  126.1 3.2 %copy-start.2 = (f32[2,1024,256]{2,1,0:T(8,128)S(1)}, f32[2,1024,256]{2,1,0:T(8,128)}, u32[]{:S(2)}) copy-start(f32[2,1024,256]{2,1,0:T(8,128)} %all-gather.5.cloned.1.call-done) | copy-start | bytes 6291460
  133.3 2.2 %copy-start = (f32[2,1024,512]{1,2,0:T(8,128)S(1)}, f32[2,1024,512]{1,2,0:T(8,128)}, u32[]{:S(2)}) copy-start(f32[2,1024,512]{1,2,0:T(8,128)} %copy.5) | copy-start | bytes 12582916
Sparse Core Ops, SparseCore 0:
  30.1 53.8 all-gather.2
  85.8 40.3 all-gather.4
where the time goes:
time: 151 us
  waiting for transfers between devices  97.7 us (65%)
  matrix products  14.7 us (10%)
  between operations  14.2 us (9%)
  local copies, waits for them, and re-layouts  11 us (7%)
  starting transfers between devices  8.45 us (6%)
  other arithmetic  4.41 us (3%)
    all_gather x1, waiting for transfers between devices, local(): window = lax.all_gather(held, 'x', axis=1, tiled=True)  45.9 us
    all_gather x1, waiting for transfers between devices, local(): block = lax.all_gather(panel, COL, axis=1, tiled=True)  37.6 us
    unnamed x12, local copies, waits for them, and re-layouts  11 us
    ppermute x1, waiting for transfers between devices, local(): piece = lax.ppermute(panel, AXES, transpose)  6.45 us
    ppermute x1, waiting for transfers between devices, local(): lax.ppermute(along_y, AXES, [pr for y in range(ny) for pr in shift(y, y,...  3.85 us
    ppermute x1, starting transfers between devices, local(): piece = lax.ppermute(panel, AXES, transpose)  3.8 us
    dot_general x1, matrix products, product_transposed(): lax.dot_general(left[0], right[0], dims, precision=hp)  3.24 us
  transfers between devices with their start and end apart: 7, of which 6 were waited for; matrix products, arithmetic and copies ran while one was open for 8% of the time, Pallas kernels for 0%

commit v1 on v0

--- a/solution.py
+++ b/solution.py
@@ -52,7 +52,9 @@
 
     def local(trailing, panel, diag_inverse):
         scaled = complex_product(panel, diag_inverse)
-        block = lax.all_gather(panel, COL, axis=1, tiled=True)
+        block = jnp.concatenate(
+            lax.all_to_all(jnp.stack([panel] * lax.axis_size(COL)), COL, 0, 0), axis=1
+        )
         yi = lax.axis_index("y")
         hi = lax.axis_index("zh")
         piece = lax.ppermute(panel, AXES, transpose)

time: 151 us -> 135 us (0.89)
  waiting for transfers between devices: 97.7 us -> 60.1 us
  starting transfers between devices: 8.45 us -> 26.9 us
  local copies, waits for them, and re-layouts: 11 us -> 13.7 us
    all_gather x1 -> x0, waiting for transfers between devices: 37.6 us -> none  [local(): block = lax.all_gather(panel, COL, axis=1, tiled=True)]
    all_gather x1, waiting for transfers between devices: 45.9 us -> 16.6 us  [local(): window = lax.all_gather(held, 'x', axis=1, tiled=True)]
    ppermute x1, waiting for transfers between devices: 3.85 us -> 31.3 us  [local(): lax.ppermute(along_y, AXES, [pr for y in range(ny) for pr in shift(y, y,...]
    all_to_all x0 -> x1, starting transfers between devices: none -> 18.5 us  [local(): lax.all_to_all(jnp.stack([panel] * lax.axis_size(COL)), COL, 0, 0)]
    ppermute x1, waiting for transfers between devices: 0.63 us -> 5.72 us  [local(): r3 = lax.ppermute(piece, AXES, shift(0, ny - 1, 0, 0))]
    ppermute x1, waiting for transfers between devices: 2.54 us -> 0.01 us  [local(): r1 = lax.ppermute(piece, AXES, shift(0, 1, 0, 0))]
    another operation x0 -> x1, local copies, waits for them, and re-layouts: none -> 2.49 us  [local(): jnp.stack([panel] * lax.axis_size(COL))]
  transfers between devices with their start and end apart: 7 -> 7, of which waited for: 6 -> 4; matrix products, arithmetic and copies ran while one was open for 8% -> 12% of each run, Pallas kernels for 0% -> 0%
where the time goes in v1:
time: 135 us; the launch traced here: 133 us
  waiting for transfers between devices  60.1 us (45%)
  starting transfers between devices  26.9 us (20%)
  between operations  14.2 us (11%)
  matrix products  14.1 us (10%)
  local copies, waits for them, and re-layouts  13.7 us (10%)
  other arithmetic  4.41 us (3%)
    ppermute x1, waiting for transfers between devices, local(): lax.ppermute(along_y, AXES, [pr for y in range(ny) for pr in shift(y, y,...  31.3 us
    all_to_all x1, starting transfers between devices, local(): lax.all_to_all(jnp.stack([panel] * lax.axis_size(COL)), COL, 0, 0)  18.5 us
    all_gather x1, waiting for transfers between devices, local(): window = lax.all_gather(held, 'x', axis=1, tiled=True)  16.6 us
    unnamed x12, local copies, waits for them, and re-layouts  11 us
    ppermute x1, waiting for transfers between devices, local(): piece = lax.ppermute(panel, AXES, transpose)  6.45 us
    ppermute x1, waiting for transfers between devices, local(): r3 = lax.ppermute(piece, AXES, shift(0, ny - 1, 0, 0))  5.72 us
    ppermute x1, starting transfers between devices, local(): piece = lax.ppermute(panel, AXES, transpose)  3.8 us
    sub x1, other arithmetic, local(): updated = trailing - product_transposed(block, tiles)  2.89 us
  transfers between devices with their start and end apart: 7, of which 4 were waited for; matrix products, arithmetic and copies ran while one was open for 12% of the time, Pallas kernels for 0%

profile of v1, /device:TPU:2, one launch (start us, length us, event | category | flops | bytes accessed | tf_op | source)
XLA Modules:
  0.0 133.4 jit_solution(4554178497953800075)
XLA Ops:
  7.2 3.8 %collective-permute-start = (f32[2,128,256]{2,1,0:T(8,128)}, f32[2,128,256]{2,1,0:T(8,128)S(1)}, u32[]{:S(2)}, u32[]{:S(2)}) collective-permute-start(f32[2,128,256]{2,1,0:T(8,128)} %param.4), channel_id=1, source_target_pairs={{0,0},{1,8},{2,16},{3,24},{4,1},{5,9},{6,17},{7,25},{8,2},{9,10},{... | collective-permute-start | bytes 786440 | tf_op jit(solution)/shard_map/ppermute | solution.py:60
  11.0 6.4 %collective-permute-done = f32[2,128,256]{2,1,0:T(8,128)S(1)} collective-permute-done((f32[2,128,256]{2,1,0:T(8,128)}, f32[2,128,256]{2,1,0:T(8,128)S(1)}, u32[]{:S(2)}, u32[]{:S(2)}) %collective-permute-start) | collective-permute-done | bytes 262176 | tf_op jit(solution)/shard_map/ppermute | solution.py:60
  17.4 1.3 collective-permute-start.1
  18.7 2.5 %stack.32 = f32[8,2,128,256]{3,2,1,0:T(8,128)} broadcast(f32[2,128,256]{2,1,0:T(8,128)} %param.4), dimensions={1,2,3} | broadcast | bytes 2359296 | tf_op jit(solution)/shard_map/stack | solution.py:56
  21.2 18.5 %all-to-all-start = ((f32[8,2,128,256]{3,2,1,0:T(8,128)}), f32[8,2,128,256]{3,2,1,0:T(8,128)S(1)}, u32[]{:S(2)}, u32[]{:S(2)}) async-start(f32[8,2,128,256]{3,2,1,0:T(8,128)} %stack.32), calls=%async_computation | async-start | bytes 4194304 | tf_op jit(solution)/shard_map/all_to_all | solution.py:56
  39.7 0.0 all-gather.2.cloned.1.call-start
  39.8 1.3 collective-permute-start.3
  41.1 0.7 collective-permute-start.2
  41.8 5.7 %collective-permute-done.3 = f32[2,128,256]{2,1,0:T(8,128)S(1)} collective-permute-done((f32[2,128,256]{2,1,0:T(8,128)S(1)}, f32[2,128,256]{2,1,0:T(8,128)S(1)}, u32[]{:S(2)}, u32[]{:S(2)}) %collective-permute-start.3) | collective-permute-done | bytes 262176 | tf_op jit(solution)/shard_map/ppermute | solution.py:62
  47.5 0.1 select_select_fusion
  47.6 1.3 collective-permute-start.4
  48.9 31.3 %collective-permute-done.4 = f32[2,128,256]{2,1,0:T(8,128)S(1)} collective-permute-done((f32[2,128,256]{2,1,0:T(8,128)S(1)}, f32[2,128,256]{2,1,0:T(8,128)S(1)}, u32[]{:S(2)}, u32[]{:S(2)}) %collective-permute-start.4) | collective-permute-done | bytes 262176 | tf_op jit(solution)/shard_map/ppermute | solution.py:65
  80.2 0.7 broadcast_select_fusion
  81.0 5.4 %copy.5 = f32[2,1024,512]{1,2,0:T(8,128)} copy(f32[2,1024,512]{2,1,0:T(8,128)} %param.3) | data formatting | bytes 8388608 | tf_op args[0]
  86.4 0.3 fusion.6
  86.7 0.3 fusion
  87.0 0.3 fusion.12
  87.3 0.3 fusion.1
  87.6 0.7 pad_maximum_fusion
  88.3 16.6 %all-gather.2.cloned.1.call-done = f32[2,512,256]{2,1,0:T(8,128)} async-done(((f32[2,128,256]{2,1,0:T(8,128)}), f32[2,512,256]{2,1,0:T(8,128)}) %all-gather.2.cloned.1.call-update) | async-done | bytes 1048592 | tf_op jit(solution)/shard_map/all_gather | solution.py:67
  104.9 1.7 %fusion.3 = f32[512,256]{1,0:T(8,128)S(1)} fusion(f32[2,512,256]{2,1,0:T(8,128)} %all-gather.2.cloned.1.call-done, f32[2,256,256]{2,1,0:T(8,128)S(1)} %copy-done.1), kind=kOutput, calls=%fused_computation.12 | convolution fusion | flops 402653184 | bytes 1310720 | tf_op jit(solution)/shard_map/dot_general | solution.py:14
  106.6 1.6 %fusion.2 = f32[512,256]{1,0:T(8,128)S(1)} fusion(f32[2,512,256]{2,1,0:T(8,128)} %all-gather.2.cloned.1.call-done, f32[2,256,256]{2,1,0:T(8,128)S(1)} %copy-done.1), kind=kOutput, calls=%fused_computation.11 | convolution fusion | flops 402653184 | bytes 1310720 | tf_op jit(solution)/shard_map/dot_general | solution.py:15
  108.2 0.6 convolution_subtract_fusion
  108.8 1.4 %convolution_add_fusion = f32[512,256]{1,0:T(8,128)} fusion(f32[512,256]{1,0:T(8,128)S(1)} %fusion.2, f32[2,512,256]{2,1,0:T(8,128)S(1)} %copy-done.3, f32[2,256,256]{2,1,0:T(8,128)S(1)} %copy-done.1), kind=kOutput, calls=%fused_computation.3 | convolution fusion | flops 402784256 | bytes 1835008 | tf_op jit(solution)/shard_map/dot_general | solution.py:15
  110.2 0.1 fusion.30
  110.4 1.9 %fusion.31 = f32[512,1024]{1,0:T(8,128)S(1)} fusion(f32[512,256]{1,0:T(8,128)S(1)} %convolution_subtract_fusion, f32[1024,256]{1,0:T(8,128)S(1)} %bitcast.59), kind=kOutput, calls=%fused_computation.43 | convolution fusion | flops 1610612736 | bytes 3670016 | tf_op jit(solution)/shard_map/dot_general | solution.py:22
  112.2 1.9 %fusion.32 = f32[512,1024]{1,0:T(8,128)S(1)} fusion(f32[512,256]{1,0:T(8,128)S(1)} %copy-done.2, f32[1024,256]{1,0:T(8,128)S(1)} %bitcast.60), kind=kOutput, calls=%fused_computation.44 | convolution fusion | flops 1610612736 | bytes 3670016 | tf_op jit(solution)/shard_map/dot_general | solution.py:25
  114.1 2.0 %subtract_bitcast_fusion = f32[1,1024,512]{1,2,0:T(8,128)S(1)} fusion(f32[512,1024]{1,0:T(8,128)S(1)} %fusion.31, f32[512,256]{1,0:T(8,128)S(1)} %copy-done.2, f32[1024,256]{1,0:T(8,128)S(1)} %bitcast.61), kind=kOutput, calls=%fused_computation.2 | convolution fusion | flops 1611137024 | bytes 5767168 | tf_op jit(solution)/shard_map/dot_general | solution.py:22
  116.1 2.0 %add_bitcast_fusion = f32[1,1024,512]{1,2,0:T(8,128)S(1)} fusion(f32[512,1024]{1,0:T(8,128)S(1)} %fusion.32, f32[512,256]{1,0:T(8,128)S(1)} %convolution_subtract_fusion, f32[1024,256]{1,0:T(8,128)S(1)} %bitcast.62), kind=kOutput, calls=%fused_computation.1 | convolution fusion | flops 1611137024 | bytes 5767168 | tf_op jit(solution)/shard_map/dot_general | solution.py:25
  118.1 0.2 copy-done
  118.3 2.9 %maximum_subtract_fusion = f32[2,1024,512]{1,2,0:T(8,128)} fusion(f32[2,1024,512]{1,2,0:T(8,128)S(1)} %copy-done, f32[1,1024,512]{1,2,0:T(8,128)S(1)} %add_bitcast_fusion, f32[1,1024,512]{1,2,0:T(8,128)S(1)} %subtract_bitcast_fusion), kind=kLoop, calls=%fused_computation | loop fusion | flops 2097152 | bytes 12582912 | tf_op jit(solution)/shard_map/sub | solution.py:69
  121.2 5.4 %copy.6 = f32[2,1024,512]{2,1,0:T(8,128)} copy(f32[2,1024,512]{1,2,0:T(8,128)} %maximum_subtract_fusion) | data formatting | bytes 8388608
  (13 shorter events, 0.0 us)
Async XLA Ops:
  7.2 10.3 %collective-permute-start = (f32[2,128,256]{2,1,0:T(8,128)}, f32[2,128,256]{2,1,0:T(8,128)S(1)}, u32[]{:S(2)}, u32[]{:S(2)}) collective-permute-start(f32[2,128,256]{2,1,0:T(8,128)} %param.4), channel_id=1, source_target_pairs={{0,0},{1,8},{2,16},{3,24},{4,1},{5,9},{6,17},{7,25},{8,2},{9,10},{... | collective-permute-start | bytes 786440 | tf_op jit(solution)/shard_map/ppermute | solution.py:60
  17.4 23.7 %collective-permute-start.1 = (f32[2,128,256]{2,1,0:T(8,128)S(1)}, f32[2,128,256]{2,1,0:T(8,128)S(1)}, u32[]{:S(2)}, u32[]{:S(2)}) collective-permute-start(f32[2,128,256]{2,1,0:T(8,128)S(1)} %collective-permute-done), channel_id=1, source_target_pairs={{0,64},{1,65},{2,66},{3,67},{4,68},{5,69},{6,70},{7,71},{8,72},{9,... | collective-permute-start | bytes 786440 | tf_op jit(solution)/shard_map/ppermute | solution.py:61
  21.2 89.0 %all-to-all-start = ((f32[8,2,128,256]{3,2,1,0:T(8,128)}), f32[8,2,128,256]{3,2,1,0:T(8,128)S(1)}, u32[]{:S(2)}, u32[]{:S(2)}) async-start(f32[8,2,128,256]{3,2,1,0:T(8,128)} %stack.32), calls=%async_computation | async-start | bytes 4194304 | tf_op jit(solution)/shard_map/all_to_all | solution.py:56
  39.7 65.1 %all-gather.2.cloned.1.call-start = ((), (), s32[]{:S(2)}) async-start(), calls=%async_computation.1 | async-start | bytes 1310720 | tf_op jit(solution)/shard_map/all_gather | solution.py:67
  39.8 7.7 %collective-permute-start.3 = (f32[2,128,256]{2,1,0:T(8,128)S(1)}, f32[2,128,256]{2,1,0:T(8,128)S(1)}, u32[]{:S(2)}, u32[]{:S(2)}) collective-permute-start(f32[2,128,256]{2,1,0:T(8,128)S(1)} %collective-permute-done), channel_id=1, source_target_pairs={{0,192},{1,193},{2,194},{3,195},{4,196},{5,197},{6,198},{7,199},{8... | collective-permute-start | bytes 786440 | tf_op jit(solution)/shard_map/ppermute | solution.py:62
  41.1 6.4 %collective-permute-start.2 = (f32[2,128,256]{2,1,0:T(8,128)S(1)}, f32[2,128,256]{2,1,0:T(8,128)S(1)}, u32[]{:S(2)}, u32[]{:S(2)}) collective-permute-start(f32[2,128,256]{2,1,0:T(8,128)S(1)} %collective-permute-done.1), channel_id=1, source_target_pairs={{64,128},{65,129},{66,130},{67,131},{68,132},{69,133},{70,134},{71... | collective-permute-start | bytes 786440 | tf_op jit(solution)/shard_map/ppermute | solution.py:63
  47.6 32.6 %collective-permute-start.4 = (f32[2,128,256]{2,1,0:T(8,128)S(1)}, f32[2,128,256]{2,1,0:T(8,128)S(1)}, u32[]{:S(2)}, u32[]{:S(2)}) collective-permute-start(f32[2,128,256]{2,1,0:T(8,128)S(1)} %select_select_fusion), channel_id=1, source_target_pairs={{0,32},{1,33},{2,34},{3,35},{4,36},{5,37},{6,38},{7,39},{8,40},{9,... | collective-permute-start | bytes 786440 | tf_op jit(solution)/shard_map/ppermute | solution.py:65
  81.0 5.5 %copy-start.1 = (f32[2,256,256]{2,1,0:T(8,128)S(1)}, f32[2,256,256]{2,1,0:T(8,128)}, u32[]{:S(2)}) copy-start(f32[2,256,256]{2,1,0:T(8,128)} %param.5) | copy-start | bytes 1572868
  81.0 5.4 %copy-start.4 = (f32[2,128,256]{2,1,0:T(8,128)S(1)}, f32[2,128,256]{2,1,0:T(8,128)}, u32[]{:S(2)}) copy-start(f32[2,128,256]{2,1,0:T(8,128)} %param.4) | copy-start | bytes 786436
  104.9 3.3 %copy-start.3 = (f32[2,512,256]{2,1,0:T(8,128)S(1)}, f32[2,512,256]{2,1,0:T(8,128)}, u32[]{:S(2)}) copy-start(f32[2,512,256]{2,1,0:T(8,128)} %all-gather.2.cloned.1.call-done) | copy-start | bytes 3145732
  110.3 1.9 %copy-start.2 = (f32[512,256]{1,0:T(8,128)S(1)}, f32[512,256]{1,0:T(8,128)}, u32[]{:S(2)}) copy-start(f32[512,256]{1,0:T(8,128)} %convolution_add_fusion) | copy-start | bytes 1572868
  116.1 2.2 %copy-start = (f32[2,1024,512]{1,2,0:T(8,128)S(1)}, f32[2,1024,512]{1,2,0:T(8,128)}, u32[]{:S(2)}) copy-start(f32[2,1024,512]{1,2,0:T(8,128)} %copy.5) | copy-start | bytes 12582916
Sparse Core Ops, SparseCore 0:
  81.1 23.7 all-gather.1
